TPU v7x, 512 devices: a whole 4x4x16 slice. The times are simulated.
512 devices in a mesh: fibre: 32 (over z, core), group: 16 (over y, x).
Axes of the slice: x: 4, y: 4, z: 16, core: 2. Of those that a mesh axis runs over, the one named last changes fastest.
Arguments:
- species_field: float32 [512, 524288], P('fibre', 'group'), may hold values from -45 to 45, as said below
- start_block: float32 [512, 64], replicated, may hold values from -4 to 4
Outputs:
- mode_basis: float32 [512, 64], replicated
- core_tensor: float32 [64, 524288], P(None, ('group', 'fibre'))
Inputs may be any that keep to these rules, and one draw needn't show every extreme that they name: `species_field`: float32 field values.
All inputs are finite; a program needn't handle non-finite values.
Results may differ from a plain program's by a relative error of at most 0.0003.
Values sent between devices are 32-bit elements; how exact they have to be, the bound alone decides.
No kernel may reach another device: no remote copies, remote signals or barrier semaphores. Data moves between devices by JAX's collectives and lax.ppermute only.
A program may use at most 64 MiB of HBM per device.

v0:
```python
import jax
import jax.numpy as jnp
from jax import lax
from jax.sharding import PartitionSpec as P

ITERS = 3
highest_precision = lax.Precision.HIGHEST


def orthonormal(matrix):
    inner_gram = jnp.dot(matrix.T, matrix, precision=highest_precision)
    lower_factor = jnp.linalg.cholesky(inner_gram)
    return lax.linalg.triangular_solve(
        lower_factor, matrix, left_side=False, lower=True, transpose_a=True
    )


def on_device(species_field, start_block):
    fibres = lax.all_to_all(species_field, "fibre", split_axis=1, concat_axis=0, tiled=True)
    total_columns = fibres.shape[1] * lax.axis_size("fibre") * lax.axis_size("group")
    mode_basis = orthonormal(start_block)
    local_gram = jnp.dot(fibres, fibres.T, precision=highest_precision) / total_columns
    gram_matrix = lax.psum(local_gram, ("fibre", "group"))
    for iteration in range(ITERS):
        mode_basis = orthonormal(jnp.dot(gram_matrix, mode_basis, precision=highest_precision))
    core_tensor = jnp.dot(mode_basis.T, fibres, precision=highest_precision)
    return (mode_basis, core_tensor)


def solution(mesh):
    placed = (P("fibre", "group"), P())
    return jax.shard_map(
        on_device,
        mesh=mesh,
        in_specs=placed,
        out_specs=(P(), P(None, ("group", "fibre"))),
        check_vma=False,
    )
```

profile of v0, /device:TPU:1, one launch (start us, length us, event | category | flops | bytes accessed | tf_op | source)
XLA Modules:
  0.0 643.5 jit_solution(7276870236529994059)
XLA Ops:
  7.2 3.2 copy.24
  10.4 16.7 %all-to-all-start = ((f32[16,32,1024]{2,0,1:T(8,128)}), f32[16,32,1024]{2,0,1:T(8,128)S(1)}, u32[]{:S(2)}, u32[]{:S(2)}) async-start(f32[16,32,1024]{2,0,1:T(8,128)} %bitcast.75), calls=%async_computation | async-start | bytes 4194304 | tf_op jit(solution)/shard_map/all_to_all | solution.py:19
  27.6 5.8 cholesky.74
  33.5 92.3 %all-to-all-done = f32[16,32,1024]{2,0,1:T(8,128)S(1)} async-done(((f32[16,32,1024]{2,0,1:T(8,128)}), f32[16,32,1024]{2,0,1:T(8,128)S(1)}, u32[]{:S(2)}, u32[]{:S(2)}) %all-to-all-start) | async-done | bytes 2097184 | tf_op jit(solution)/shard_map/all_to_all | solution.py:19
  125.8 4.6 convolution_multiply_fusion
  131.0 0.7 fusion
  131.6 4.9 custom-call.8
  136.9 454.4 %all-reduce.2.cloned.1.call-done = f32[512,512]{1,0:T(8,128)} async-done(((f32[512,512]{1,0:T(8,128)}), f32[512,512]{1,0:T(8,128)}) %all-reduce.2.cloned.1.call-update) | async-done | bytes 1048592 | tf_op jit(solution)/shard_map/psum | solution.py:23
  591.3 2.4 fusion.19
  594.1 5.8 cholesky.85
  600.0 0.6 compare_reduce_fusion.2
  600.6 0.7 fusion.1
  601.3 4.9 custom-call.9
  606.5 1.1 fusion.21
  608.0 5.8 cholesky.96
  613.9 0.6 compare_reduce_fusion.1
  614.5 0.7 fusion.2
  615.2 4.9 custom-call.10
  620.4 1.3 fusion.23
  622.1 5.8 cholesky.107
  628.0 0.6 compare_reduce_fusion
  628.6 0.7 fusion.3
  629.3 4.9 custom-call.11
  634.6 2.1 fusion.25
  (29 shorter events, 3.6 us)
Async XLA Ops:
  7.2 20.0 %copy-start = (f32[512,64]{0,1:T(8,128)S(1)}, f32[512,64]{0,1:T(8,128)}, u32[]{:S(2)}) copy-start(f32[512,64]{0,1:T(8,128)} %param.6) | copy-start | bytes 393220
  10.4 115.4 %all-to-all-start = ((f32[16,32,1024]{2,0,1:T(8,128)}), f32[16,32,1024]{2,0,1:T(8,128)S(1)}, u32[]{:S(2)}, u32[]{:S(2)}) async-start(f32[16,32,1024]{2,0,1:T(8,128)} %bitcast.75), calls=%async_computation | async-start | bytes 4194304 | tf_op jit(solution)/shard_map/all_to_all | solution.py:19
  27.2 564.1 %all-reduce.2.cloned.1.call-start = ((), (), s32[]{:S(2)}) async-start(), calls=%async_computation.1 | async-start | bytes 2097152 | tf_op jit(solution)/shard_map/psum | solution.py:23
  591.3 15.2 %copy-start.1 = (f32[512,512]{1,0:T(8,128)S(1)}, f32[512,512]{1,0:T(8,128)}, u32[]{:S(2)}) copy-start(f32[512,512]{1,0:T(8,128)} %all-reduce.2.cloned.1.call-done) | copy-start | bytes 3145732
  634.5 2.1 copy-start.2
Sparse Core Ops, SparseCore 0:
  130.5 460.7 all-reduce.1
where the time goes:
time: 644 us; the launch traced here: 643 us
  waiting for transfers between devices  547 us (85%)
  other arithmetic  48.3 us (8%)
  starting transfers between devices  16.8 us (3%)
  between operations  14.2 us (2%)
  matrix products  13.9 us (2%)
    psum x1, waiting for transfers between devices, on_device(): gram_matrix = lax.psum(local_gram, ('fibre', 'group'))  454 us
    all_to_all x1, waiting for transfers between devices, on_device(): lax.all_to_all(species_field, 'fibre', split_axis=1, concat_axis=0, tiled...  92.3 us
    another operation x12, other arithmetic, orthonormal(): lower_factor = jnp.linalg.cholesky(inner_gram)  26.1 us
    another operation x8, other arithmetic, orthonormal(): lax.linalg.triangular_solve(lower_factor, matrix, left_side=False, lower=...  22.2 us
    all_to_all x1, starting transfers between devices, on_device(): lax.all_to_all(species_field, 'fibre', split_axis=1, concat_axis=0, tiled...  16.7 us
  transfers between devices with their start and end apart: 2, of which 2 were waited for; matrix products, arithmetic and copies ran while one was open for 2% of the time, Pallas kernels for 0%

commit v1 on v0

--- a/solution.py
+++ b/solution.py
@@ -20,7 +20,13 @@
     total_columns = fibres.shape[1] * lax.axis_size("fibre") * lax.axis_size("group")
     mode_basis = orthonormal(start_block)
     local_gram = jnp.dot(fibres, fibres.T, precision=highest_precision) / total_columns
-    gram_matrix = lax.psum(local_gram, ("fibre", "group"))
+
+    def test_sample(point, ax_name, a_name):
+        for no in (ax_name, a_name):
+            point = jax.lax.psum(point, no)
+        return point
+
+    gram_matrix = test_sample(local_gram, "group", "fibre")
     for iteration in range(ITERS):
         mode_basis = orthonormal(jnp.dot(gram_matrix, mode_basis, precision=highest_precision))
     core_tensor = jnp.dot(mode_basis.T, fibres, precision=highest_precision)

time: 644 us -> 505 us (0.78)
  waiting for transfers between devices: 547 us -> 309 us
  blocking collectives: 0 us -> 117 us
  starting transfers between devices: 16.8 us -> 0.26 us
    psum x1 -> x2, waiting for transfers between devices: 454 us -> 308 us  [test_sample(): point = jax.lax.psum(point, no)]
    all_to_all x0 -> x1, blocking collectives: none -> 117 us  [on_device(): lax.all_to_all(species_field, 'fibre', split_axis=1, concat_axis=0, tiled...]
    all_to_all x1 -> x0, waiting for transfers between devices: 92.3 us -> none  [on_device(): lax.all_to_all(species_field, 'fibre', split_axis=1, concat_axis=0, tiled...]
    all_to_all x1 -> x0, starting transfers between devices: 16.7 us -> none  [on_device(): lax.all_to_all(species_field, 'fibre', split_axis=1, concat_axis=0, tiled...]
  transfers between devices with their start and end apart: 2 -> 2, of which waited for: 2 -> 2; matrix products, arithmetic and copies ran while one was open for 2% -> 3% of each run, Pallas kernels for 0% -> 0%
where the time goes in v1:
time: 505 us; the launch traced here: 504 us
  waiting for transfers between devices  309 us (61%)
  blocking collectives  117 us (23%)
  other arithmetic  48.3 us (10%)
  between operations  14.2 us (3%)
  matrix products  13.8 us (3%)
    psum x2, waiting for transfers between devices, test_sample(): point = jax.lax.psum(point, no)  308 us
    all_to_all x1, blocking collectives, on_device(): lax.all_to_all(species_field, 'fibre', split_axis=1, concat_axis=0, tiled...  117 us
    another operation x12, other arithmetic, orthonormal(): lower_factor = jnp.linalg.cholesky(inner_gram)  26.1 us
    another operation x8, other arithmetic, orthonormal(): lax.linalg.triangular_solve(lower_factor, matrix, left_side=False, lower=...  22.2 us
  transfers between devices with their start and end apart: 2, of which 2 were waited for; matrix products, arithmetic and copies ran while one was open for 3% of the time, Pallas kernels for 0%

profile of v1, /device:TPU:1, one launch (start us, length us, event | category | flops | bytes accessed | tf_op | source)
XLA Modules:
  0.0 504.4 jit_solution(1205673229309258222)
XLA Ops:
  7.2 1.8 copy.24
  9.0 117.2 %all_to_all.19 = f32[16,32,1024]{2,0,1:T(8,128)S(1)} all-to-all(f32[16,32,1024]{2,0,1:T(8,128)S(1)} %bitcast.75), channel_id=1, replica_groups=mesh['fibre'=32,'group'=16] {'fibre'}, dimensions={1} | all-to-all | bytes 4194304 | tf_op jit(solution)/shard_map/all_to_all | solution.py:19
  126.2 4.6 convolution_multiply_fusion
  131.4 5.8 %cholesky.74 = f32[64,64]{1,0:T(8,128)S(1)} custom-call(f32[64,64]{1,0:T(8,128)S(1)} %fusion.11), custom_call_target="Cholesky" | custom-call | tf_op jit(solution)/shard_map/jit(cholesky)/cholesky | solution.py:12
  137.3 101.7 %all-reduce.3.cloned.1.call-done = f32[512,512]{1,0:T(8,128)} async-done(((f32[512,512]{1,0:T(8,128)}), f32[512,512]{1,0:T(8,128)}) %all-reduce.3.cloned.1.call-update) | async-done | bytes 1048592 | tf_op jit(solution)/shard_map/psum | solution.py:26
  239.6 0.7 fusion
  240.3 4.9 custom-call.8
  245.5 206.8 %all-reduce.5.cloned.1.call-done = f32[512,512]{1,0:T(8,128)} async-done(((f32[512,512]{1,0:T(8,128)}), f32[512,512]{1,0:T(8,128)}) %all-reduce.5.cloned.1.call-update) | async-done | bytes 1048592 | tf_op jit(solution)/shard_map/psum | solution.py:26
  452.3 2.4 fusion.19
  455.1 5.8 %cholesky.85 = f32[64,64]{1,0:T(8,128)S(1)} custom-call(f32[64,64]{1,0:T(8,128)S(1)} %fusion.9), custom_call_target="Cholesky" | custom-call | tf_op jit(solution)/shard_map/jit(cholesky)/cholesky | solution.py:12
  461.0 0.6 compare_reduce_fusion.2
  461.6 0.7 fusion.1
  462.3 4.9 custom-call.9
  467.6 1.1 fusion.21
  469.0 5.8 %cholesky.96 = f32[64,64]{1,0:T(8,128)S(1)} custom-call(f32[64,64]{1,0:T(8,128)S(1)} %fusion.7), custom_call_target="Cholesky" | custom-call | tf_op jit(solution)/shard_map/jit(cholesky)/cholesky | solution.py:12
  474.9 0.6 compare_reduce_fusion.1
  475.6 0.7 fusion.2
  476.2 4.9 custom-call.10
  481.5 1.1 fusion.23
  483.0 5.8 %cholesky.107 = f32[64,64]{1,0:T(8,128)S(1)} custom-call(f32[64,64]{1,0:T(8,128)S(1)} %fusion.5), custom_call_target="Cholesky" | custom-call | tf_op jit(solution)/shard_map/jit(cholesky)/cholesky | solution.py:12
  488.9 0.6 compare_reduce_fusion
  489.5 0.7 fusion.3
  490.2 4.9 custom-call.11
  495.4 2.1 fusion.25
  (31 shorter events, 3.8 us)
Async XLA Ops:
  7.2 123.9 %copy-start = (f32[512,64]{0,1:T(8,128)S(1)}, f32[512,64]{0,1:T(8,128)}, u32[]{:S(2)}) copy-start(f32[512,64]{0,1:T(8,128)} %param.6) | copy-start | bytes 393220
  7.2 231.8 %all-reduce.3.cloned.1.call-start = ((), (), s32[]{:S(2)}) async-start(), calls=%async_computation.1 | async-start | bytes 2097152 | tf_op jit(solution)/shard_map/psum | solution.py:26
  130.8 321.5 %all-reduce.5.cloned.1.call-start = ((), (), s32[]{:S(2)}) async-start(), calls=%async_computation.2 | async-start | bytes 2097152 | tf_op jit(solution)/shard_map/psum | solution.py:26
  452.3 15.2 %copy-start.1 = (f32[512,512]{1,0:T(8,128)S(1)}, f32[512,512]{1,0:T(8,128)}, u32[]{:S(2)}) copy-start(f32[512,512]{1,0:T(8,128)} %all-reduce.5.cloned.1.call-done) | copy-start | bytes 3145732
  495.4 2.1 copy-start.2
Sparse Core Ops, SparseCore 0:
  130.9 107.9 all-reduce.2
  241.3 210.9 all-reduce.4
